TPU v7x, 32 devices: a whole 2x2x4 slice. The times are simulated.
32 devices in a mesh: gx: 8 (over z, x), gy: 4 (over y, core).
Axes of the slice: x: 2, y: 2, z: 4, core: 2. Of those that a mesh axis runs over, the one named last changes fastest.
Arguments:
- patches: bfloat16 [128, 64, 256], P('gx', 'gy'), may hold values from -9 to 9
- w_query: bfloat16 [256, 256], replicated, may hold values from -2 to 2
- w_key: bfloat16 [256, 256], replicated, may hold values from -2 to 2
- w_value: bfloat16 [256, 256], replicated, may hold values from -0.375 to 0.375
- w_out: bfloat16 [256, 256], replicated, may hold values from -0.375 to 0.375
- region_memory: bfloat16 [8, 4, 4, 64, 512], P('gx', 'gy'), may hold values from -6 to 6
- region_owner: int32 [8, 4, 4, 2], P('gx', 'gy'), may hold values from 0 to 7, all different within a row; in each aligned block of 4 rows (0 to 3, 4 to 7, ..., all dimensions but the last counted through in order) at most 2 rows name the same one
- region_local: int32 [8, 4, 4, 2], P('gx', 'gy'), may hold values from 0 to 3
- grad_out: bfloat16 [128, 64, 256], P('gx', 'gy'), may hold values from -6 to 6
Outputs:
- layer_out: bfloat16 [128, 64, 256], P('gx', 'gy')
- grad_patches: bfloat16 [128, 64, 256], P('gx', 'gy')
- grad_w_query: float32 [256, 256], replicated
- grad_w_key: float32 [256, 256], replicated
- grad_w_value: float32 [256, 256], replicated
- grad_w_out: float32 [256, 256], replicated
Inputs may be any that keep to these rules, and one draw needn't show every extreme that they name: `region_owner`: each block names two different owner tiles. The blocks of one tile name one owner at most 2 times, a bound that some tile reaches.
All inputs are finite; a program needn't handle non-finite values.
Results may differ from a plain program's by a relative error of at most 0.02.
Values may be sent and summed in bfloat16 or wider, within the bound.
No kernel may reach another device: no remote copies, remote signals or barrier semaphores. Data moves between devices by JAX's collectives and lax.ppermute only.
A program may use at most 64 MiB of HBM per device.

v0:
```python
import math
import jax
import jax.numpy as jnp
from jax import lax
from jax.sharding import PartitionSpec as P

D = 256
HEADS = 2
HEAD_DIM = 128
BSIDE = 8
BT = 64
masked_score = -1000000000.0


def padded(block, sides, width):
    for axis, dim in sides:
        count = lax.axis_size(axis)
        forward = [(i, i + 1) for i in range(count - 1)]
        backward = [(target, source) for source, target in forward]
        low = lax.ppermute(
            lax.slice_in_dim(block, block.shape[dim] - width, None, axis=dim), axis, forward
        )
        high = lax.ppermute(lax.slice_in_dim(block, 0, width, axis=dim), axis, backward)
        block = jnp.concatenate([low, block, high], axis=dim)
    return block


def to_blocks(grid_array):
    grid_rows, grid_cols, feature_width = grid_array.shape
    shaped = grid_array.reshape(grid_rows // BSIDE, BSIDE, grid_cols // BSIDE, BSIDE, feature_width)
    return shaped.transpose(0, 2, 1, 3, 4).reshape(
        grid_rows // BSIDE, grid_cols // BSIDE, BSIDE * BSIDE, feature_width
    )


def from_blocks(block_array):
    block_rows, block_cols, block_tokens, feature_width = block_array.shape
    shaped = block_array.reshape(block_rows, block_cols, BSIDE, BSIDE, feature_width)
    return shaped.transpose(0, 2, 1, 3, 4).reshape(
        block_rows * BSIDE, block_cols * BSIDE, feature_width
    )


def split_heads(source):
    return source.reshape(source.shape[:-1] + (HEADS, source.shape[-1] // HEADS))


def key_pieces(keyval_pad, key_valid, region_keyval):
    block_rows, block_cols = (region_keyval.shape[0], region_keyval.shape[1])
    pieces = []
    for row_off in range(3):
        for col_off in range(3):
            key_block = keyval_pad[row_off : row_off + block_rows, col_off : col_off + block_cols]
            valid_mask = key_valid[row_off : row_off + block_rows, col_off : col_off + block_cols]
            pieces.append((key_block[..., :D], key_block[..., D:], valid_mask))
    merged = region_keyval.reshape(block_rows, block_cols, 2 * BT, 2 * D)
    pieces.append(
        (merged[..., :D], merged[..., D:], jnp.ones((block_rows, block_cols), dtype=jnp.bool_))
    )
    return pieces


def piece_scores(query_heads, key_part, valid_mask):
    scores = jnp.einsum(
        "abqhe,abkhe->abhqk", query_heads, split_heads(key_part), preferred_element_type=jnp.float32
    )
    scores = scores * (1.0 / math.sqrt(HEAD_DIM))
    return jnp.where(valid_mask[:, :, None, None, None], scores, masked_score)


def attend_forward(query_blocks, keyval_pad, key_valid, region_keyval):
    query_heads = split_heads(query_blocks)
    pieces = key_pieces(keyval_pad, key_valid, region_keyval)
    scores = [
        piece_scores(query_heads, key_part, valid_mask)
        for key_part, value_part, valid_mask in pieces
    ]
    row_top = jnp.max(jnp.concatenate(scores, -1), -1, keepdims=True)
    row_total = sum(
        (jnp.sum(jnp.exp(part_scores - row_top), -1, keepdims=True) for part_scores in scores)
    )
    log_total = row_top + jnp.log(row_total)
    mixed_sum = jnp.zeros(query_heads.shape, jnp.float32)
    for part_scores, (key_part, value_part, valid_mask) in zip(scores, pieces):
        weights = jnp.exp(part_scores - log_total).astype(jnp.bfloat16)
        mixed_sum = mixed_sum + jnp.einsum(
            "abhqk,abkhe->abqhe",
            weights,
            split_heads(value_part),
            preferred_element_type=jnp.float32,
        )
    output = mixed_sum.reshape(query_blocks.shape).astype(jnp.bfloat16)
    return (output, log_total[..., 0])


def query_grads(
    query_blocks, keyval_pad, key_valid, region_keyval, log_total, dout_blocks, delta_rows
):
    query_heads = split_heads(query_blocks)
    dout_heads = split_heads(dout_blocks)
    accum_sum = jnp.zeros(query_heads.shape, jnp.float32)
    for key_part, value_part, valid_mask in key_pieces(keyval_pad, key_valid, region_keyval):
        part_scores = piece_scores(query_heads, key_part, valid_mask)
        prob_part = jnp.exp(part_scores - log_total[..., None])
        grad_prob = jnp.einsum(
            "abqhe,abkhe->abhqk",
            dout_heads,
            split_heads(value_part),
            preferred_element_type=jnp.float32,
        )
        grad_score = (prob_part * (grad_prob - delta_rows[..., None])).astype(jnp.bfloat16)
        accum_sum = accum_sum + jnp.einsum(
            "abhqk,abkhe->abqhe",
            grad_score,
            split_heads(key_part),
            preferred_element_type=jnp.float32,
        )
    return (
        (accum_sum * (1.0 / math.sqrt(HEAD_DIM))).reshape(query_blocks.shape).astype(jnp.bfloat16)
    )


def key_grads(keyval_center, query_pad, dout_pad, log_pad, delta_pad, query_valid):
    block_rows, block_cols = (keyval_center.shape[0], keyval_center.shape[1])
    key_heads = split_heads(keyval_center[..., :D])
    value_heads = split_heads(keyval_center[..., D:])
    grad_key = jnp.zeros(key_heads.shape, jnp.float32)
    grad_value = jnp.zeros(key_heads.shape, jnp.float32)
    for row_off in range(3):
        for col_off in range(3):
            query_heads = split_heads(
                query_pad[row_off : row_off + block_rows, col_off : col_off + block_cols]
            )
            dout_heads = split_heads(
                dout_pad[row_off : row_off + block_rows, col_off : col_off + block_cols]
            )
            log_part = log_pad[row_off : row_off + block_rows, col_off : col_off + block_cols]
            delta_part = delta_pad[row_off : row_off + block_rows, col_off : col_off + block_cols]
            valid_mask = query_valid[row_off : row_off + block_rows, col_off : col_off + block_cols]
            part_scores = jnp.einsum(
                "abqhe,abkhe->abhqk", query_heads, key_heads, preferred_element_type=jnp.float32
            )
            part_scores = part_scores * (1.0 / math.sqrt(HEAD_DIM))
            prob_part = jnp.where(
                valid_mask[:, :, None, None, None], jnp.exp(part_scores - log_part[..., None]), 0.0
            )
            grad_prob = jnp.einsum(
                "abqhe,abkhe->abhqk", dout_heads, value_heads, preferred_element_type=jnp.float32
            )
            grad_score = (prob_part * (grad_prob - delta_part[..., None])).astype(jnp.bfloat16)
            grad_key = grad_key + jnp.einsum(
                "abhqk,abqhe->abkhe", grad_score, query_heads, preferred_element_type=jnp.float32
            )
            rounded_prob = prob_part.astype(jnp.bfloat16)
            grad_value = grad_value + jnp.einsum(
                "abhqk,abqhe->abkhe", rounded_prob, dout_heads, preferred_element_type=jnp.float32
            )
    out_shape = (block_rows, block_cols, BT, D)
    grad_key = (grad_key * (1.0 / math.sqrt(HEAD_DIM))).reshape(out_shape).astype(jnp.bfloat16)
    return (grad_key, grad_value.reshape(out_shape).astype(jnp.bfloat16))


def inner_rows(left_rows, right_rows):
    return lax.dot_general(
        left_rows, right_rows, (((0,), (0,)), ((), ())), preferred_element_type=jnp.float32
    )


def on_device(
    patches, w_query, w_key, w_value, w_out, region_memory, region_owner, region_local, grad_out
):
    tile_rows, tile_cols, model_width = patches.shape
    block_rows, block_cols = (tile_rows // BSIDE, tile_cols // BSIDE)
    block_count = block_rows * block_cols
    flat_in = patches.reshape(-1, model_width)
    w_pair = jnp.concatenate([w_key, w_value], 1)
    queries = jnp.dot(flat_in, w_query, preferred_element_type=jnp.float32).astype(jnp.bfloat16)
    keyvals = jnp.dot(flat_in, w_pair, preferred_element_type=jnp.float32).astype(jnp.bfloat16)
    keyvals = keyvals.reshape(tile_rows, tile_cols, 2 * model_width)
    keyval_grid = padded(keyvals, (("gx", 0), ("gy", 1)), BSIDE)
    keyval_pad = to_blocks(keyval_grid)
    gx_count = lax.axis_size("gx")
    gy_count = lax.axis_size("gy")
    row_ids = lax.axis_index("gx") * block_rows - 1 + jnp.arange(block_rows + 2, dtype=jnp.int32)
    col_ids = lax.axis_index("gy") * block_cols - 1 + jnp.arange(block_cols + 2, dtype=jnp.int32)
    row_valid = (row_ids >= 0) & (row_ids < block_rows * gx_count)
    col_valid = (col_ids >= 0) & (col_ids < block_cols * gy_count)
    key_valid = row_valid[:, None] & col_valid[None, :]
    owners = region_owner.reshape(2 * block_count)
    local_ids = region_local.reshape(2 * block_count)
    memory_local = region_memory.reshape(
        region_memory.shape[2], region_memory.shape[3], region_memory.shape[4]
    )
    region_count = memory_local.shape[0]
    row_tables = lax.all_gather(memory_local, "gx", axis=0, tiled=True)
    fetched = jnp.take(row_tables, owners * region_count + local_ids, axis=0)
    region_keyval = fetched.reshape(
        block_rows, block_cols, 2, memory_local.shape[1], memory_local.shape[2]
    )
    query_blocks = to_blocks(queries.reshape(tile_rows, tile_cols, model_width))
    outputs, log_totals = attend_forward(query_blocks, keyval_pad, key_valid, region_keyval)
    attended = from_blocks(outputs).reshape(-1, model_width)
    layer_out = jnp.dot(attended, w_out, preferred_element_type=jnp.float32).astype(jnp.bfloat16)
    grad_flat = grad_out.reshape(-1, model_width)
    d_attended = jnp.dot(grad_flat, w_out.T, preferred_element_type=jnp.float32).astype(
        jnp.bfloat16
    )
    grad_out_local = inner_rows(attended, grad_flat)
    dout_blocks = to_blocks(d_attended.reshape(tile_rows, tile_cols, model_width))
    delta_rows = jnp.sum(
        split_heads(dout_blocks).astype(jnp.float32) * split_heads(outputs).astype(jnp.float32), -1
    )
    delta_rows = delta_rows.transpose(0, 1, 3, 2)
    d_queries = query_grads(
        query_blocks, keyval_pad, key_valid, region_keyval, log_totals, dout_blocks, delta_rows
    )
    query_grid = jnp.concatenate(
        [
            queries.reshape(tile_rows, tile_cols, model_width),
            d_attended.reshape(tile_rows, tile_cols, model_width),
        ],
        -1,
    )
    query_halo = padded(query_grid, (("gx", 0), ("gy", 1)), BSIDE)
    stat_grid = from_blocks(jnp.concatenate([log_totals, delta_rows], 2).transpose(0, 1, 3, 2))
    stat_halo = padded(stat_grid, (("gx", 0), ("gy", 1)), BSIDE)
    query_all = to_blocks(query_halo)
    stat_pad = to_blocks(stat_halo).transpose(0, 1, 3, 2)
    d_keys, d_values = key_grads(
        keyval_pad[1:-1, 1:-1],
        query_all[..., :model_width],
        query_all[..., model_width:],
        stat_pad[:, :, :HEADS],
        stat_pad[:, :, HEADS:],
        key_valid,
    )
    dq_flat = from_blocks(d_queries).reshape(-1, model_width)
    dk_flat = from_blocks(d_keys).reshape(-1, model_width)
    dv_flat = from_blocks(d_values).reshape(-1, model_width)
    grads_joined = jnp.concatenate([dq_flat, dk_flat, dv_flat], 1)
    w_stacked = jnp.concatenate([w_query.T, w_key.T, w_value.T], 0)
    grad_patches = jnp.dot(grads_joined, w_stacked, preferred_element_type=jnp.float32).astype(
        jnp.bfloat16
    )
    summed = lax.psum(
        (
            inner_rows(flat_in, dq_flat),
            inner_rows(flat_in, dk_flat),
            inner_rows(flat_in, dv_flat),
            grad_out_local,
        ),
        ("gx", "gy"),
    )
    return (
        layer_out.reshape(tile_rows, tile_cols, model_width),
        grad_patches.reshape(tile_rows, tile_cols, model_width),
        summed[0],
        summed[1],
        summed[2],
        summed[3],
    )


def solution(mesh):
    return jax.shard_map(
        on_device,
        mesh=mesh,
        in_specs=(
            P("gx", "gy", None),
            P(),
            P(),
            P(),
            P(),
            P("gx", "gy", None, None, None),
            P("gx", "gy", None, None),
            P("gx", "gy", None, None),
            P("gx", "gy", None),
        ),
        out_specs=(P("gx", "gy", None), P("gx", "gy", None), P(), P(), P(), P()),
        check_vma=False,
    )
```

profile of v0, /device:TPU:0, one launch (start us, length us, event | category | flops | bytes accessed | tf_op | source)
XLA Modules:
  0.0 271.7 jit_solution(11771590287470757042)
XLA Ops:
  10.6 5.5 %collective-permute-start = (bf16[8,16,512]{2,1,0:T(8,128)(2,1)S(1)}, bf16[8,16,512]{2,1,0:T(8,128)(2,1)S(1)}, u32[]{:S(2)}, u32[]{:S(2)}) collective-permute-start(bf16[8,16,512]{2,1,0:T(8,128)(2,1)S(1)} %bitcast.503), channel_id=1, source_target_pairs={{0,4},{4,8},{8,12},{12,16},{16,20},{20,24},{24,28},{1,5},{5,9},{9,... | collective-permute-start | bytes 393224 | tf_op jit(solution)/shard_map/ppermute | solution.py:20
  18.4 4.8 %collective-permute-start.4 = (bf16[8,16,512]{2,1,0:T(8,128)(2,1)S(1)}, bf16[8,16,512]{2,1,0:T(8,128)(2,1)S(1)}, u32[]{:S(2)}, u32[]{:S(2)}) collective-permute-start(bf16[8,16,512]{2,1,0:T(8,128)(2,1)S(1)} %get-tuple-element.85), channel_id=1, source_target_pairs={{0,4},{4,8},{8,12},{12,16},{16,20},{20,24},{24,28},{1,5},{5,9},{9,... | collective-permute-start | bytes 393224 | tf_op jit(solution)/shard_map/ppermute | solution.py:20
  25.1 3.5 %collective-permute-done.4 = bf16[8,16,512]{2,1,0:T(8,128)(2,1)S(1)} collective-permute-done((bf16[8,16,512]{2,1,0:T(8,128)(2,1)S(1)}, bf16[8,16,512]{2,1,0:T(8,128)(2,1)S(1)}, u32[]{:S(2)}, u32[]{:S(2)}) %collective-permute-start.4) | collective-permute-done | bytes 131104 | tf_op jit(solution)/shard_map/ppermute | solution.py:20
  28.6 1.5 collective-permute-done.5
  33.0 4.8 %collective-permute-start.2 = (bf16[32,8,512]{2,1,0:T(8,128)(2,1)S(1)}, bf16[32,8,512]{2,1,0:T(8,128)(2,1)S(1)}, u32[]{:S(2)}, u32[]{:S(2)}) collective-permute-start(bf16[32,8,512]{2,1,0:T(8,128)(2,1)S(1)} %get-tuple-element.83), channel_id=1, source_target_pairs={{0,1},{1,2},{2,3},{4,5},{5,6},{6,7},{8,9},{9,10},{10,11},{12,13},{... | collective-permute-start | bytes 786440 | tf_op jit(solution)/shard_map/ppermute | solution.py:20
  39.7 2.8 %collective-permute-done.3 = bf16[32,8,512]{2,1,0:T(8,128)(2,1)} collective-permute-done((bf16[32,8,512]{2,1,0:T(8,128)(2,1)S(1)}, bf16[32,8,512]{2,1,0:T(8,128)(2,1)}, u32[]{:S(2)}, u32[]{:S(2)}) %collective-permute-start.3) | collective-permute-done | bytes 262176 | tf_op jit(solution)/shard_map/ppermute | solution.py:23
  50.2 1.5 slice_bitcast_fusion
  51.7 13.7 %all-gather.3.cloned.1.call-done = bf16[1,1,32,64,512]{4,3,1,0,2:T(8,128)(2,1)} async-done(((bf16[1,1,4,64,512]{4,3,1,0,2:T(8,128)(2,1)}), bf16[1,1,32,64,512]{4,3,1,0,2:T(8,128)(2,1)}) %all-gather.3.cloned.1.call-update) | async-done | bytes 2097168 | tf_op jit(solution)/shard_map/all_gather | solution.py:195
  65.4 2.2 gather_fusion
  75.2 2.1 fusion.84
  77.3 2.2 convolution_add_fusion.24
  79.5 2.2 convolution_add_fusion.23
  88.7 2.4 collective-permute-start.8
  94.3 4.7 %collective-permute-done.9 = f32[8,16,4]{1,0,2:T(8,128)S(1)} collective-permute-done((f32[8,16,4]{1,0,2:T(8,128)S(1)}, f32[8,16,4]{1,0,2:T(8,128)S(1)}, u32[]{:S(2)}, u32[]{:S(2)}) %collective-permute-start.9) | collective-permute-done | bytes 2080 | tf_op jit(solution)/shard_map/ppermute | solution.py:23
  100.3 1.5 collective-permute-start.11
  102.8 2.4 collective-permute-done.11
  111.9 1.6 convert_element_type.219
  113.5 1.6 copy.530
  115.1 2.0 convolution_add_fusion.15
  127.3 130.5 %all-reduce.3.cloned.1.call-done = (f32[256,256]{0,1:T(8,128)}, f32[256,256]{0,1:T(8,128)}, f32[256,256]{0,1:T(8,128)}, f32[256,256]{1,0:T(8,128)}) async-done(((f32[256,256]{0,1:T(8,128)}, f32[256,256]{0,1:T(8,128)}, f32[256,256]{0,1:T(8,128)}, f32[256,256]{1,0:T(8,128)}), (f32[256,256]{0,1:T(8,128)}, f32[256,256]{0,1:T(8,128)}, f32[256,256]{0,1:T(8,128)}, ...) | async-done | bytes 1048592 | tf_op jit(solution)/shard_map/psum | solution.py:245
  257.8 1.8 copy.531
  259.6 1.8 copy.532
  261.4 1.8 copy.533
  263.2 1.7 copy.1109
  (302 shorter events, 55.3 us)
Async XLA Ops:
  7.2 17.4 %copy-start.59 = (s32[1,1,4,2]{2,3,1,0:T(2,128)S(1)}, s32[1,1,4,2]{2,3,1,0:T(2,128)}, u32[]{:S(2)}) copy-start(s32[1,1,4,2]{2,3,1,0:T(2,128)} %param.16) | copy-start | bytes 100
  7.2 58.2 %all-gather.3.cloned.1.call-start = ((), (), s32[]{:S(2)}) async-start(), calls=%async_computation | async-start | bytes 2359296 | tf_op jit(solution)/shard_map/all_gather | solution.py:195
  7.9 249.9 %all-reduce.3.cloned.1.call-start = ((), (), s32[]{:S(2)}) async-start(), calls=%async_computation.1 | async-start | bytes 2097152 | tf_op jit(solution)/shard_map/psum | solution.py:245
  9.3 23.5 %collective-permute-start.1 = (bf16[8,16,512]{2,1,0:T(8,128)(2,1)S(1)}, bf16[8,16,512]{2,1,0:T(8,128)(2,1)S(1)}, u32[]{:S(2)}, u32[]{:S(2)}) collective-permute-start(bf16[8,16,512]{2,1,0:T(8,128)(2,1)S(1)} %bitcast.504), channel_id=1, source_target_pairs={{4,0},{8,4},{12,8},{16,12},{20,16},{24,20},{28,24},{5,1},{9,5},{13... | collective-permute-start | bytes 393224 | tf_op jit(solution)/shard_map/ppermute | solution.py:23
  10.6 22.2 %collective-permute-start = (bf16[8,16,512]{2,1,0:T(8,128)(2,1)S(1)}, bf16[8,16,512]{2,1,0:T(8,128)(2,1)S(1)}, u32[]{:S(2)}, u32[]{:S(2)}) collective-permute-start(bf16[8,16,512]{2,1,0:T(8,128)(2,1)S(1)} %bitcast.503), channel_id=1, source_target_pairs={{0,4},{4,8},{8,12},{12,16},{16,20},{20,24},{24,28},{1,5},{5,9},{9,... | collective-permute-start | bytes 393224 | tf_op jit(solution)/shard_map/ppermute | solution.py:20
  18.4 10.2 %collective-permute-start.4 = (bf16[8,16,512]{2,1,0:T(8,128)(2,1)S(1)}, bf16[8,16,512]{2,1,0:T(8,128)(2,1)S(1)}, u32[]{:S(2)}, u32[]{:S(2)}) collective-permute-start(bf16[8,16,512]{2,1,0:T(8,128)(2,1)S(1)} %get-tuple-element.85), channel_id=1, source_target_pairs={{0,4},{4,8},{8,12},{12,16},{16,20},{20,24},{24,28},{1,5},{5,9},{9,... | collective-permute-start | bytes 393224 | tf_op jit(solution)/shard_map/ppermute | solution.py:20
  23.2 6.9 %collective-permute-start.5 = (bf16[8,16,512]{2,1,0:T(8,128)(2,1)S(1)}, bf16[8,16,512]{2,1,0:T(8,128)(2,1)S(1)}, u32[]{:S(2)}, u32[]{:S(2)}) collective-permute-start(bf16[8,16,512]{2,1,0:T(8,128)(2,1)S(1)} %get-tuple-element.86), channel_id=1, source_target_pairs={{4,0},{8,4},{12,8},{16,12},{20,16},{24,20},{28,24},{5,1},{9,5},{13... | collective-permute-start | bytes 393224 | tf_op jit(solution)/shard_map/ppermute | solution.py:23
  25.0 20.0 %copy-start.75 = (pred[2,2]{1,0:T(4,128)(4,1)}, pred[2,2]{1,0:T(4,128)(4,1)S(1)}, u32[]{:S(2)}) copy-start(pred[2,2]{1,0:T(4,128)(4,1)S(1)} %get-tuple-element.112) | copy-start | bytes 16
  25.0 20.3 %copy-start.73 = (pred[2,2]{1,0:T(4,128)(4,1)}, pred[2,2]{1,0:T(4,128)(4,1)S(1)}, u32[]{:S(2)}) copy-start(pred[2,2]{1,0:T(4,128)(4,1)S(1)} %get-tuple-element.113) | copy-start | bytes 16
  25.0 20.5 %copy-start.71 = (pred[2,2]{1,0:T(4,128)(4,1)}, pred[2,2]{1,0:T(4,128)(4,1)S(1)}, u32[]{:S(2)}) copy-start(pred[2,2]{1,0:T(4,128)(4,1)S(1)} %get-tuple-element.114) | copy-start | bytes 16
  25.0 20.7 %copy-start.69 = (pred[2,2]{1,0:T(4,128)(4,1)}, pred[2,2]{1,0:T(4,128)(4,1)S(1)}, u32[]{:S(2)}) copy-start(pred[2,2]{1,0:T(4,128)(4,1)S(1)} %get-tuple-element.115) | copy-start | bytes 16
  25.0 20.9 %copy-start.65 = (pred[2,2]{1,0:T(4,128)(4,1)}, pred[2,2]{1,0:T(4,128)(4,1)S(1)}, u32[]{:S(2)}) copy-start(pred[2,2]{1,0:T(4,128)(4,1)S(1)} %get-tuple-element.117) | copy-start | bytes 16
  25.0 21.8 %copy-start.63 = (pred[2,2]{1,0:T(4,128)(4,1)}, pred[2,2]{1,0:T(4,128)(4,1)S(1)}, u32[]{:S(2)}) copy-start(pred[2,2]{1,0:T(4,128)(4,1)S(1)} %get-tuple-element.118) | copy-start | bytes 16
  25.1 22.6 %copy-start.61 = (pred[2,2]{1,0:T(4,128)(4,1)}, pred[2,2]{1,0:T(4,128)(4,1)S(1)}, u32[]{:S(2)}) copy-start(pred[2,2]{1,0:T(4,128)(4,1)S(1)} %get-tuple-element.111) | copy-start | bytes 16
  25.1 23.4 %copy-start.77 = (pred[2,2]{1,0:T(4,128)(4,1)}, pred[2,2]{1,0:T(4,128)(4,1)S(1)}, u32[]{:S(2)}) copy-start(pred[2,2]{1,0:T(4,128)(4,1)S(1)} %get-tuple-element.119) | copy-start | bytes 16
  25.1 24.3 %copy-start.67 = (pred[2,2]{1,0:T(4,128)(4,1)}, pred[2,2]{1,0:T(4,128)(4,1)S(1)}, u32[]{:S(2)}) copy-start(pred[2,2]{1,0:T(4,128)(4,1)S(1)} %get-tuple-element.116) | copy-start | bytes 16
  30.2 9.3 %collective-permute-start.6 = (bf16[32,8,512]{2,1,0:T(8,128)(2,1)S(1)}, bf16[32,8,512]{2,1,0:T(8,128)(2,1)S(1)}, u32[]{:S(2)}, u32[]{:S(2)}) collective-permute-start(bf16[32,8,512]{2,1,0:T(8,128)(2,1)S(1)} %get-tuple-element.79), channel_id=1, source_target_pairs={{0,1},{1,2},{2,3},{4,5},{5,6},{6,7},{8,9},{9,10},{10,11},{12,13},{... | collective-permute-start | bytes 786440 | tf_op jit(solution)/shard_map/ppermute | solution.py:20
  31.5 8.0 %collective-permute-start.7 = (bf16[32,8,512]{2,1,0:T(8,128)(2,1)S(1)}, bf16[32,8,512]{2,1,0:T(8,128)(2,1)S(1)}, u32[]{:S(2)}, u32[]{:S(2)}) collective-permute-start(bf16[32,8,512]{2,1,0:T(8,128)(2,1)S(1)} %get-tuple-element.80), channel_id=1, source_target_pairs={{1,0},{2,1},{3,2},{5,4},{6,5},{7,6},{9,8},{10,9},{11,10},{13,12},{... | collective-permute-start | bytes 786440 | tf_op jit(solution)/shard_map/ppermute | solution.py:23
  33.0 6.8 %collective-permute-start.2 = (bf16[32,8,512]{2,1,0:T(8,128)(2,1)S(1)}, bf16[32,8,512]{2,1,0:T(8,128)(2,1)S(1)}, u32[]{:S(2)}, u32[]{:S(2)}) collective-permute-start(bf16[32,8,512]{2,1,0:T(8,128)(2,1)S(1)} %get-tuple-element.83), channel_id=1, source_target_pairs={{0,1},{1,2},{2,3},{4,5},{5,6},{6,7},{8,9},{9,10},{10,11},{12,13},{... | collective-permute-start | bytes 786440 | tf_op jit(solution)/shard_map/ppermute | solution.py:20
  37.7 4.8 %collective-permute-start.3 = (bf16[32,8,512]{2,1,0:T(8,128)(2,1)S(1)}, bf16[32,8,512]{2,1,0:T(8,128)(2,1)}, u32[]{:S(2)}, u32[]{:S(2)}) collective-permute-start(bf16[32,8,512]{2,1,0:T(8,128)(2,1)S(1)} %get-tuple-element.84), channel_id=1, source_target_pairs={{1,0},{2,1},{3,2},{5,4},{6,5},{7,6},{9,8},{10,9},{11,10},{13,12},{... | collective-permute-start | bytes 786440 | tf_op jit(solution)/shard_map/ppermute | solution.py:23
  88.7 5.5 %collective-permute-start.8 = (f32[8,16,4]{1,0,2:T(8,128)S(1)}, f32[8,16,4]{1,0,2:T(8,128)S(1)}, u32[]{:S(2)}, u32[]{:S(2)}) collective-permute-start(f32[8,16,4]{1,0,2:T(8,128)S(1)} %slice.401), channel_id=1, source_target_pairs={{0,4},{4,8},{8,12},{12,16},{16,20},{20,24},{24,28},{1,5},{5,9},{9,... | collective-permute-start | bytes 6152 | tf_op jit(solution)/shard_map/ppermute | solution.py:20
  93.0 6.0 %collective-permute-start.9 = (f32[8,16,4]{1,0,2:T(8,128)S(1)}, f32[8,16,4]{1,0,2:T(8,128)S(1)}, u32[]{:S(2)}, u32[]{:S(2)}) collective-permute-start(f32[8,16,4]{1,0,2:T(8,128)S(1)} %slice.403), channel_id=1, source_target_pairs={{4,0},{8,4},{12,8},{16,12},{20,16},{24,20},{28,24},{5,1},{9,5},{13... | collective-permute-start | bytes 6152 | tf_op jit(solution)/shard_map/ppermute | solution.py:23
  99.0 3.7 %collective-permute-start.10 = (f32[32,8,4]{1,0,2:T(8,128)S(1)}, f32[32,8,4]{1,0,2:T(8,128)S(1)}, u32[]{:S(2)}, u32[]{:S(2)}) collective-permute-start(f32[32,8,4]{1,0,2:T(8,128)S(1)} %get-tuple-element.89), channel_id=1, source_target_pairs={{0,1},{1,2},{2,3},{4,5},{5,6},{6,7},{8,9},{9,10},{10,11},{12,13},{... | collective-permute-start | bytes 12296 | tf_op jit(solution)/shard_map/ppermute | solution.py:20
  100.3 4.8 %collective-permute-start.11 = (f32[32,8,4]{1,0,2:T(8,128)S(1)}, f32[32,8,4]{1,0,2:T(8,128)S(1)}, u32[]{:S(2)}, u32[]{:S(2)}) collective-permute-start(f32[32,8,4]{1,0,2:T(8,128)S(1)} %get-tuple-element.90), channel_id=1, source_target_pairs={{1,0},{2,1},{3,2},{5,4},{6,5},{7,6},{9,8},{10,9},{11,10},{13,12},{... | collective-permute-start | bytes 12296 | tf_op jit(solution)/shard_map/ppermute | solution.py:23
  (69 other events, 277.6 us)
Sparse Core Ops, SparseCore 0:
  10.2 55.1 all-gather.2
  125.6 132.2 all-reduce.2
where the time goes:
time: 273 us; the launch traced here: 272 us
  waiting for transfers between devices  160 us (59%)
  matrix products  44.2 us (16%)
  starting transfers between devices  28.1 us (10%)
  local copies, waits for them, and re-layouts  20.5 us (8%)
  between operations  15.9 us (6%)
  other arithmetic  3.19 us (1%)
    psum x1, waiting for transfers between devices, on_device(): lax.psum((inner_rows(flat_in, dq_flat), inner_rows(flat_in, dk_flat), inn...  131 us
    ppermute x6, starting transfers between devices, padded(): lax.ppermute(lax.slice_in_dim(block, block.shape[dim] - width, None, axis...  20.1 us
    all_gather x1, waiting for transfers between devices, on_device(): row_tables = lax.all_gather(memory_local, 'gx', axis=0, tiled=True)  13.7 us
    dot_general x10, matrix products, query_grads(): jnp.einsum('abhqk,abkhe->abqhe', grad_score, split_heads(key_part), prefe...  13.1 us
    ppermute x6, waiting for transfers between devices, padded(): lax.ppermute(lax.slice_in_dim(block, 0, width, axis=dim), axis, backward)  11.4 us
    unnamed x166, local copies, waits for them, and re-layouts  10.8 us
    dot_general x9, matrix products, key_grads(): jnp.einsum('abhqk,abqhe->abkhe', grad_score, query_heads, preferred_eleme...  8.38 us
    ppermute x6, starting transfers between devices, padded(): lax.ppermute(lax.slice_in_dim(block, 0, width, axis=dim), axis, backward)  7.92 us
  transfers between devices with their start and end apart: 14, of which 7 were waited for; matrix products, arithmetic and copies ran while one was open for 7% of the time, Pallas kernels for 0%

commit v1 on v0

--- a/solution.py
+++ b/solution.py
@@ -10,6 +10,15 @@
 BSIDE = 8
 BT = 64
 masked_score = -1000000000.0
+
+
+def grid_guide(tile_in, along_dim):
+    tile_in = jnp.moveaxis(tile_in, 0, along_dim)
+    big = tile_in.shape
+    part_now = tile_in.reshape(
+        *big[:along_dim], big[along_dim] * big[along_dim + 1], *big[along_dim + 2 :]
+    )
+    return part_now
 
 
 def padded(block, sides, width):
@@ -192,7 +201,25 @@
         region_memory.shape[2], region_memory.shape[3], region_memory.shape[4]
     )
     region_count = memory_local.shape[0]
-    row_tables = lax.all_gather(memory_local, "gx", axis=0, tiled=True)
+    how_many = lax.axis_size("gx")
+    log = [(w, (w + 1) % how_many) for w in range(how_many)]
+    grid = [(s, ix) for ix, s in log]
+    block_out, then = ([], [])
+    for dev_i in range(how_many - 1):
+        if dev_i % 2 == 0:
+            moved = lax.ppermute(
+                block_out[-1] if block_out else memory_local, axis_name="gx", perm=log
+            )
+            block_out.append(moved)
+        else:
+            piece_now = lax.ppermute(then[-1] if then else memory_local, "gx", perm=grid)
+            then.append(piece_now)
+    current_value = jnp.stack([*block_out[::-1], memory_local, *then])
+    f_now = lax.axis_index("gx")
+    v1 = len(block_out)
+    y1 = f_now - v1
+    current_value = current_value[(jnp.arange(how_many) - y1) % how_many]
+    row_tables = grid_guide(current_value, 0)
     fetched = jnp.take(row_tables, owners * region_count + local_ids, axis=0)
     region_keyval = fetched.reshape(
         block_rows, block_cols, 2, memory_local.shape[1], memory_local.shape[2]

time: 273 us -> 301 us (1.10)
  matrix products: 44.2 us -> 58.9 us
  starting transfers between devices: 28.1 us -> 41.4 us
  waiting for transfers between devices: 160 us -> 152 us
  local copies, waits for them, and re-layouts: 20.5 us -> 28.3 us
    ppermute x0 -> x7, starting transfers between devices: none -> 19.1 us  [the longest x3 9.73 us: on_device(): lax.ppermute(then[-1] if then else memory_local, 'gx', perm=grid)]
    all_gather x1 -> x0, waiting for transfers between devices: 13.7 us -> none  [on_device(): row_tables = lax.all_gather(memory_local, 'gx', axis=0, tiled=True)]
    ppermute x0 -> x7, waiting for transfers between devices: none -> 11.3 us  [the longest x4 11.3 us: on_device(): lax.ppermute(block_out[-1] if block_out else memory_local, axis_name='gx'...]
    dot_general x9, matrix products: 8.38 us -> 16.7 us  [key_grads(): jnp.einsum('abhqk,abqhe->abkhe', grad_score, query_heads, preferred_eleme...]
    ppermute x6, starting transfers between devices: 20.1 us -> 14.4 us  [padded(): lax.ppermute(lax.slice_in_dim(block, block.shape[dim] - width, None, axis...]
    unnamed x166 -> x181, local copies, waits for them, and re-layouts: 10.8 us -> 15.9 us
    dot_general x10, matrix products: 6.23 us -> 10.5 us  [piece_scores(): jnp.einsum('abqhe,abkhe->abhqk', query_heads, split_heads(key_part), pref...]
    ppermute x6, waiting for transfers between devices: 11.4 us -> 8.01 us  [padded(): lax.ppermute(lax.slice_in_dim(block, 0, width, axis=dim), axis, backward)]
  transfers between devices with their start and end apart: 14 -> 20, of which waited for: 7 -> 7; matrix products, arithmetic and copies ran while one was open for 7% -> 9% of each run, Pallas kernels for 0% -> 0%
where the time goes in v1:
time: 301 us; the launch traced here: 300 us
  waiting for transfers between devices  152 us (50%)
  matrix products  58.9 us (20%)
  starting transfers between devices  41.4 us (14%)
  local copies, waits for them, and re-layouts  28.3 us (9%)
  between operations  15.7 us (5%)
  other arithmetic  3.45 us (1%)
    psum x1, waiting for transfers between devices, on_device(): lax.psum((inner_rows(flat_in, dq_flat), inner_rows(flat_in, dk_flat), inn...  130 us
    dot_general x9, matrix products, key_grads(): jnp.einsum('abhqk,abqhe->abkhe', grad_score, query_heads, preferred_eleme...  16.7 us
    unnamed x181, local copies, waits for them, and re-layouts  15.9 us
    ppermute x6, starting transfers between devices, padded(): lax.ppermute(lax.slice_in_dim(block, block.shape[dim] - width, None, axis...  14.4 us
    dot_general x10, matrix products, query_grads(): jnp.einsum('abhqk,abkhe->abqhe', grad_score, split_heads(key_part), prefe...  13.1 us
    ppermute x4, waiting for transfers between devices, on_device(): lax.ppermute(block_out[-1] if block_out else memory_local, axis_name='gx'...  11.3 us
    dot_general x10, matrix products, piece_scores(): jnp.einsum('abqhe,abkhe->abhqk', query_heads, split_heads(key_part), pref...  10.5 us
    ppermute x3, starting transfers between devices, on_device(): lax.ppermute(then[-1] if then else memory_local, 'gx', perm=grid)  9.73 us
  transfers between devices with their start and end apart: 20, of which 7 were waited for; matrix products, arithmetic and copies ran while one was open for 9% of the time, Pallas kernels for 0%

profile of v1, /device:TPU:0, one launch (start us, length us, event | category | flops | bytes accessed | tf_op | source)
XLA Modules:
  0.0 300.1 jit_solution(463458870912633536)
XLA Ops:
  7.2 3.0 collective-permute-start.4
  10.2 3.1 %collective-permute-start.8 = (bf16[4,64,512]{2,1,0:T(8,128)(2,1)}, bf16[4,64,512]{2,1,0:T(8,128)(2,1)S(1)}, u32[]{:S(2)}, u32[]{:S(2)}) collective-permute-start(bf16[4,64,512]{2,1,0:T(8,128)(2,1)} %bitcast.517), channel_id=1, source_target_pairs={{4,0},{8,4},{12,8},{16,12},{20,16},{24,20},{28,24},{0,28},{5,1},{9... | collective-permute-start | bytes 786440 | tf_op jit(solution)/shard_map/ppermute | solution.py:215
  19.5 4.6 %collective-permute-start.11 = (bf16[8,16,512]{2,1,0:T(8,128)(2,1)S(1)}, bf16[8,16,512]{2,1,0:T(8,128)(2,1)S(1)}, u32[]{:S(2)}, u32[]{:S(2)}) collective-permute-start(bf16[8,16,512]{2,1,0:T(8,128)(2,1)S(1)} %get-tuple-element.79), channel_id=1, source_target_pairs={{0,4},{4,8},{8,12},{12,16},{16,20},{20,24},{24,28},{1,5},{5,9},{9,... | collective-permute-start | bytes 393224 | tf_op jit(solution)/shard_map/ppermute | solution.py:29
  25.1 3.3 %collective-permute-done = bf16[8,16,512]{2,1,0:T(8,128)(2,1)S(1)} collective-permute-done((bf16[8,16,512]{2,1,0:T(8,128)(2,1)S(1)}, bf16[8,16,512]{2,1,0:T(8,128)(2,1)S(1)}, u32[]{:S(2)}, u32[]{:S(2)}) %collective-permute-start) | collective-permute-done | bytes 131104 | tf_op jit(solution)/shard_map/ppermute | solution.py:29
  32.4 3.3 %collective-permute-done.12 = bf16[8,16,512]{2,1,0:T(8,128)(2,1)S(1)} collective-permute-done((bf16[8,16,512]{2,1,0:T(8,128)(2,1)S(1)}, bf16[8,16,512]{2,1,0:T(8,128)(2,1)S(1)}, u32[]{:S(2)}, u32[]{:S(2)}) %collective-permute-start.12) | collective-permute-done | bytes 131104 | tf_op jit(solution)/shard_map/ppermute | solution.py:32
  38.7 3.2 %collective-permute-start.5 = (bf16[4,64,512]{2,1,0:T(8,128)(2,1)S(1)}, bf16[4,64,512]{2,1,0:T(8,128)(2,1)S(1)}, u32[]{:S(2)}, u32[]{:S(2)}) collective-permute-start(bf16[4,64,512]{2,1,0:T(8,128)(2,1)S(1)} %collective-permute-done.4), channel_id=1, source_target_pairs={{0,4},{4,8},{8,12},{12,16},{16,20},{20,24},{24,28},{28,0},{1,5},{5... | collective-permute-start | bytes 786440 | tf_op jit(solution)/shard_map/ppermute | solution.py:210
  51.9 3.2 %collective-permute-start.6 = (bf16[4,64,512]{2,1,0:T(8,128)(2,1)S(1)}, bf16[4,64,512]{2,1,0:T(8,128)(2,1)S(1)}, u32[]{:S(2)}, u32[]{:S(2)}) collective-permute-start(bf16[4,64,512]{2,1,0:T(8,128)(2,1)S(1)} %collective-permute-done.5), channel_id=1, source_target_pairs={{0,4},{4,8},{8,12},{12,16},{16,20},{20,24},{24,28},{28,0},{1,5},{5... | collective-permute-start | bytes 786440 | tf_op jit(solution)/shard_map/ppermute | solution.py:210
  58.1 6.0 %collective-permute-done.6 = bf16[4,64,512]{2,1,0:T(8,128)(2,1)S(1)} collective-permute-done((bf16[4,64,512]{2,1,0:T(8,128)(2,1)S(1)}, bf16[4,64,512]{2,1,0:T(8,128)(2,1)S(1)}, u32[]{:S(2)}, u32[]{:S(2)}) %collective-permute-start.6) | collective-permute-done | bytes 262176 | tf_op jit(solution)/shard_map/ppermute | solution.py:210
  66.5 4.7 %collective-permute-start.10 = (bf16[4,64,512]{2,1,0:T(8,128)(2,1)S(1)}, bf16[4,64,512]{2,1,0:T(8,128)(2,1)S(1)}, u32[]{:S(2)}, u32[]{:S(2)}) collective-permute-start(bf16[4,64,512]{2,1,0:T(8,128)(2,1)S(1)} %collective-permute-done.9), channel_id=1, source_target_pairs={{4,0},{8,4},{12,8},{16,12},{20,16},{24,20},{28,24},{0,28},{5,1},{9... | collective-permute-start | bytes 786440 | tf_op jit(solution)/shard_map/ppermute | solution.py:215
  71.2 5.2 %collective-permute-done.7 = bf16[4,64,512]{2,1,0:T(8,128)(2,1)S(1)} collective-permute-done((bf16[4,64,512]{2,1,0:T(8,128)(2,1)S(1)}, bf16[4,64,512]{2,1,0:T(8,128)(2,1)S(1)}, u32[]{:S(2)}, u32[]{:S(2)}) %collective-permute-start.7) | collective-permute-done | bytes 262176 | tf_op jit(solution)/shard_map/ppermute | solution.py:210
  82.3 2.3 gather_fusion
  94.7 2.1 fusion.84
  96.8 2.2 convolution_add_fusion.24
  99.0 2.2 convolution_add_fusion.23
  108.6 4.5 %collective-permute-start.15 = (f32[8,16,4]{1,0,2:T(8,128)S(1)}, f32[8,16,4]{1,0,2:T(8,128)S(1)}, u32[]{:S(2)}, u32[]{:S(2)}) collective-permute-start(f32[8,16,4]{1,0,2:T(8,128)S(1)} %slice.401), channel_id=1, source_target_pairs={{0,4},{4,8},{8,12},{12,16},{16,20},{20,24},{24,28},{1,5},{5,9},{9,... | collective-permute-start | bytes 6152 | tf_op jit(solution)/shard_map/ppermute | solution.py:29
  115.9 4.0 %collective-permute-done.16 = f32[8,16,4]{1,0,2:T(8,128)S(1)} collective-permute-done((f32[8,16,4]{1,0,2:T(8,128)S(1)}, f32[8,16,4]{1,0,2:T(8,128)S(1)}, u32[]{:S(2)}, u32[]{:S(2)}) %collective-permute-start.16) | collective-permute-done | bytes 2080 | tf_op jit(solution)/shard_map/ppermute | solution.py:32
  132.3 2.2 convolution_add_fusion.14
  134.5 2.1 convolution_add_fusion.13
  136.6 2.1 convolution_add_fusion.12
  138.7 2.0 convolution_add_fusion.11
  140.7 2.0 convolution_add_fusion.10
  142.8 2.0 convolution_add_fusion.9
  144.8 2.0 fusion.81
  156.6 129.6 %all-reduce.3.cloned.1.call-done = (f32[256,256]{0,1:T(8,128)}, f32[256,256]{0,1:T(8,128)}, f32[256,256]{0,1:T(8,128)}, f32[256,256]{1,0:T(8,128)}) async-done(((f32[256,256]{0,1:T(8,128)}, f32[256,256]{0,1:T(8,128)}, f32[256,256]{0,1:T(8,128)}, f32[256,256]{1,0:T(8,128)}), (f32[256,256]{0,1:T(8,128)}, f32[256,256]{0,1:T(8,128)}, f32[256,256]{0,1:T(8,128)}, ...) | async-done | bytes 1048592 | tf_op jit(solution)/shard_map/psum | solution.py:272
  (332 shorter events, 83.4 us)
Async XLA Ops:
  7.2 279.0 %all-reduce.3.cloned.1.call-start = ((), (), s32[]{:S(2)}) async-start(), calls=%async_computation | async-start | bytes 2097152 | tf_op jit(solution)/shard_map/psum | solution.py:272
  7.2 30.1 %collective-permute-start.4 = (bf16[4,64,512]{2,1,0:T(8,128)(2,1)}, bf16[4,64,512]{2,1,0:T(8,128)(2,1)S(1)}, u32[]{:S(2)}, u32[]{:S(2)}) collective-permute-start(bf16[4,64,512]{2,1,0:T(8,128)(2,1)} %bitcast.516), channel_id=1, source_target_pairs={{0,4},{4,8},{8,12},{12,16},{16,20},{20,24},{24,28},{28,0},{1,5},{5... | collective-permute-start | bytes 786440 | tf_op jit(solution)/shard_map/ppermute | solution.py:210
  10.2 28.4 %collective-permute-start.8 = (bf16[4,64,512]{2,1,0:T(8,128)(2,1)}, bf16[4,64,512]{2,1,0:T(8,128)(2,1)S(1)}, u32[]{:S(2)}, u32[]{:S(2)}) collective-permute-start(bf16[4,64,512]{2,1,0:T(8,128)(2,1)} %bitcast.517), channel_id=1, source_target_pairs={{4,0},{8,4},{12,8},{16,12},{20,16},{24,20},{28,24},{0,28},{5,1},{9... | collective-permute-start | bytes 786440 | tf_op jit(solution)/shard_map/ppermute | solution.py:215
  14.6 13.8 %collective-permute-start = (bf16[8,16,512]{2,1,0:T(8,128)(2,1)S(1)}, bf16[8,16,512]{2,1,0:T(8,128)(2,1)S(1)}, u32[]{:S(2)}, u32[]{:S(2)}) collective-permute-start(bf16[8,16,512]{2,1,0:T(8,128)(2,1)S(1)} %bitcast.523), channel_id=1, source_target_pairs={{0,4},{4,8},{8,12},{12,16},{16,20},{20,24},{24,28},{1,5},{5,9},{9,... | collective-permute-start | bytes 393224 | tf_op jit(solution)/shard_map/ppermute | solution.py:29
  15.9 13.8 %collective-permute-start.1 = (bf16[8,16,512]{2,1,0:T(8,128)(2,1)S(1)}, bf16[8,16,512]{2,1,0:T(8,128)(2,1)S(1)}, u32[]{:S(2)}, u32[]{:S(2)}) collective-permute-start(bf16[8,16,512]{2,1,0:T(8,128)(2,1)S(1)} %bitcast.522), channel_id=1, source_target_pairs={{4,0},{8,4},{12,8},{16,12},{20,16},{24,20},{28,24},{5,1},{9,5},{13... | collective-permute-start | bytes 393224 | tf_op jit(solution)/shard_map/ppermute | solution.py:32
  19.5 11.6 %collective-permute-start.11 = (bf16[8,16,512]{2,1,0:T(8,128)(2,1)S(1)}, bf16[8,16,512]{2,1,0:T(8,128)(2,1)S(1)}, u32[]{:S(2)}, u32[]{:S(2)}) collective-permute-start(bf16[8,16,512]{2,1,0:T(8,128)(2,1)S(1)} %get-tuple-element.79), channel_id=1, source_target_pairs={{0,4},{4,8},{8,12},{12,16},{16,20},{20,24},{24,28},{1,5},{5,9},{9,... | collective-permute-start | bytes 393224 | tf_op jit(solution)/shard_map/ppermute | solution.py:29
  24.5 32.1 %copy-start.77 = (pred[2,2]{1,0:T(4,128)(4,1)}, pred[2,2]{1,0:T(4,128)(4,1)S(1)}, u32[]{:S(2)}) copy-start(pred[2,2]{1,0:T(4,128)(4,1)S(1)} %get-tuple-element.112) | copy-start | bytes 16
  24.5 39.6 %copy-start.79 = (pred[2,2]{1,0:T(4,128)(4,1)}, pred[2,2]{1,0:T(4,128)(4,1)S(1)}, u32[]{:S(2)}) copy-start(pred[2,2]{1,0:T(4,128)(4,1)S(1)} %get-tuple-element.105) | copy-start | bytes 16
  24.5 41.1 %copy-start.81 = (pred[2,2]{1,0:T(4,128)(4,1)}, pred[2,2]{1,0:T(4,128)(4,1)S(1)}, u32[]{:S(2)}) copy-start(pred[2,2]{1,0:T(4,128)(4,1)S(1)} %get-tuple-element.113) | copy-start | bytes 16
  24.7 40.9 %copy-start.49 = (bf16[2,2,64,2,128]{4,3,2,1,0:T(2,128)(2,1)}, bf16[2,2,64,2,128]{4,3,2,1,0:T(2,128)(2,1)S(1)}, u32[]{:S(2)}) copy-start(bf16[2,2,64,2,128]{4,3,2,1,0:T(2,128)(2,1)S(1)} %reshape_reshape.29) | copy-start | bytes 393220
  28.4 7.3 %collective-permute-start.12 = (bf16[8,16,512]{2,1,0:T(8,128)(2,1)S(1)}, bf16[8,16,512]{2,1,0:T(8,128)(2,1)S(1)}, u32[]{:S(2)}, u32[]{:S(2)}) collective-permute-start(bf16[8,16,512]{2,1,0:T(8,128)(2,1)S(1)} %get-tuple-element.80), channel_id=1, source_target_pairs={{4,0},{8,4},{12,8},{16,12},{20,16},{24,20},{28,24},{5,1},{9,5},{13... | collective-permute-start | bytes 393224 | tf_op jit(solution)/shard_map/ppermute | solution.py:32
  29.8 12.0 %collective-permute-start.2 = (bf16[32,8,512]{2,1,0:T(8,128)(2,1)S(1)}, bf16[32,8,512]{2,1,0:T(8,128)(2,1)S(1)}, u32[]{:S(2)}, u32[]{:S(2)}) collective-permute-start(bf16[32,8,512]{2,1,0:T(8,128)(2,1)S(1)} %get-tuple-element.77), channel_id=1, source_target_pairs={{0,1},{1,2},{2,3},{4,5},{5,6},{6,7},{8,9},{9,10},{10,11},{12,13},{... | collective-permute-start | bytes 786440 | tf_op jit(solution)/shard_map/ppermute | solution.py:29
  31.1 12.6 %collective-permute-start.3 = (bf16[32,8,512]{2,1,0:T(8,128)(2,1)S(1)}, bf16[32,8,512]{2,1,0:T(8,128)(2,1)S(1)}, u32[]{:S(2)}, u32[]{:S(2)}) collective-permute-start(bf16[32,8,512]{2,1,0:T(8,128)(2,1)S(1)} %get-tuple-element.78), channel_id=1, source_target_pairs={{1,0},{2,1},{3,2},{5,4},{6,5},{7,6},{9,8},{10,9},{11,10},{13,12},{... | collective-permute-start | bytes 786440 | tf_op jit(solution)/shard_map/ppermute | solution.py:32
  35.8 9.4 %collective-permute-start.13 = (bf16[32,8,512]{2,1,0:T(8,128)(2,1)S(1)}, bf16[32,8,512]{2,1,0:T(8,128)(2,1)S(1)}, u32[]{:S(2)}, u32[]{:S(2)}) collective-permute-start(bf16[32,8,512]{2,1,0:T(8,128)(2,1)S(1)} %get-tuple-element.73), channel_id=1, source_target_pairs={{0,1},{1,2},{2,3},{4,5},{5,6},{6,7},{8,9},{9,10},{10,11},{12,13},{... | collective-permute-start | bytes 786440 | tf_op jit(solution)/shard_map/ppermute | solution.py:29
  37.3 7.9 %collective-permute-start.14 = (bf16[32,8,512]{2,1,0:T(8,128)(2,1)S(1)}, bf16[32,8,512]{2,1,0:T(8,128)(2,1)S(1)}, u32[]{:S(2)}, u32[]{:S(2)}) collective-permute-start(bf16[32,8,512]{2,1,0:T(8,128)(2,1)S(1)} %get-tuple-element.74), channel_id=1, source_target_pairs={{1,0},{2,1},{3,2},{5,4},{6,5},{7,6},{9,8},{10,9},{11,10},{13,12},{... | collective-permute-start | bytes 786440 | tf_op jit(solution)/shard_map/ppermute | solution.py:32
  38.7 13.2 %collective-permute-start.5 = (bf16[4,64,512]{2,1,0:T(8,128)(2,1)S(1)}, bf16[4,64,512]{2,1,0:T(8,128)(2,1)S(1)}, u32[]{:S(2)}, u32[]{:S(2)}) collective-permute-start(bf16[4,64,512]{2,1,0:T(8,128)(2,1)S(1)} %collective-permute-done.4), channel_id=1, source_target_pairs={{0,4},{4,8},{8,12},{12,16},{16,20},{20,24},{24,28},{28,0},{1,5},{5... | collective-permute-start | bytes 786440 | tf_op jit(solution)/shard_map/ppermute | solution.py:210
  41.8 24.6 %collective-permute-start.9 = (bf16[4,64,512]{2,1,0:T(8,128)(2,1)S(1)}, bf16[4,64,512]{2,1,0:T(8,128)(2,1)S(1)}, u32[]{:S(2)}, u32[]{:S(2)}) collective-permute-start(bf16[4,64,512]{2,1,0:T(8,128)(2,1)S(1)} %collective-permute-done.8), channel_id=1, source_target_pairs={{4,0},{8,4},{12,8},{16,12},{20,16},{24,20},{28,24},{0,28},{5,1},{9... | collective-permute-start | bytes 786440 | tf_op jit(solution)/shard_map/ppermute | solution.py:215
  51.9 12.2 %collective-permute-start.6 = (bf16[4,64,512]{2,1,0:T(8,128)(2,1)S(1)}, bf16[4,64,512]{2,1,0:T(8,128)(2,1)S(1)}, u32[]{:S(2)}, u32[]{:S(2)}) collective-permute-start(bf16[4,64,512]{2,1,0:T(8,128)(2,1)S(1)} %collective-permute-done.5), channel_id=1, source_target_pairs={{0,4},{4,8},{8,12},{12,16},{16,20},{20,24},{24,28},{28,0},{1,5},{5... | collective-permute-start | bytes 786440 | tf_op jit(solution)/shard_map/ppermute | solution.py:210
  64.1 12.3 %collective-permute-start.7 = (bf16[4,64,512]{2,1,0:T(8,128)(2,1)S(1)}, bf16[4,64,512]{2,1,0:T(8,128)(2,1)S(1)}, u32[]{:S(2)}, u32[]{:S(2)}) collective-permute-start(bf16[4,64,512]{2,1,0:T(8,128)(2,1)S(1)} %collective-permute-done.6), channel_id=1, source_target_pairs={{0,4},{4,8},{8,12},{12,16},{16,20},{20,24},{24,28},{28,0},{1,5},{5... | collective-permute-start | bytes 786440 | tf_op jit(solution)/shard_map/ppermute | solution.py:210
  66.5 15.1 %collective-permute-start.10 = (bf16[4,64,512]{2,1,0:T(8,128)(2,1)S(1)}, bf16[4,64,512]{2,1,0:T(8,128)(2,1)S(1)}, u32[]{:S(2)}, u32[]{:S(2)}) collective-permute-start(bf16[4,64,512]{2,1,0:T(8,128)(2,1)S(1)} %collective-permute-done.9), channel_id=1, source_target_pairs={{4,0},{8,4},{12,8},{16,12},{20,16},{24,20},{28,24},{0,28},{5,1},{9... | collective-permute-start | bytes 786440 | tf_op jit(solution)/shard_map/ppermute | solution.py:215
  108.6 7.3 %collective-permute-start.15 = (f32[8,16,4]{1,0,2:T(8,128)S(1)}, f32[8,16,4]{1,0,2:T(8,128)S(1)}, u32[]{:S(2)}, u32[]{:S(2)}) collective-permute-start(f32[8,16,4]{1,0,2:T(8,128)S(1)} %slice.401), channel_id=1, source_target_pairs={{0,4},{4,8},{8,12},{12,16},{16,20},{20,24},{24,28},{1,5},{5,9},{9,... | collective-permute-start | bytes 6152 | tf_op jit(solution)/shard_map/ppermute | solution.py:29
  114.3 5.6 %collective-permute-start.16 = (f32[8,16,4]{1,0,2:T(8,128)S(1)}, f32[8,16,4]{1,0,2:T(8,128)S(1)}, u32[]{:S(2)}, u32[]{:S(2)}) collective-permute-start(f32[8,16,4]{1,0,2:T(8,128)S(1)} %slice.403), channel_id=1, source_target_pairs={{4,0},{8,4},{12,8},{16,12},{20,16},{24,20},{28,24},{5,1},{9,5},{13... | collective-permute-start | bytes 6152 | tf_op jit(solution)/shard_map/ppermute | solution.py:32
  120.0 3.7 %collective-permute-start.17 = (f32[32,8,4]{1,0,2:T(8,128)S(1)}, f32[32,8,4]{1,0,2:T(8,128)S(1)}, u32[]{:S(2)}, u32[]{:S(2)}) collective-permute-start(f32[32,8,4]{1,0,2:T(8,128)S(1)} %get-tuple-element.83), channel_id=1, source_target_pairs={{0,1},{1,2},{2,3},{4,5},{5,6},{6,7},{8,9},{9,10},{10,11},{12,13},{... | collective-permute-start | bytes 12296 | tf_op jit(solution)/shard_map/ppermute | solution.py:29
  121.3 3.1 %collective-permute-start.18 = (f32[32,8,4]{1,0,2:T(8,128)S(1)}, f32[32,8,4]{1,0,2:T(8,128)S(1)}, u32[]{:S(2)}, u32[]{:S(2)}) collective-permute-start(f32[32,8,4]{1,0,2:T(8,128)S(1)} %get-tuple-element.84), channel_id=1, source_target_pairs={{1,0},{2,1},{3,2},{5,4},{6,5},{7,6},{9,8},{10,9},{11,10},{13,12},{... | collective-permute-start | bytes 12296 | tf_op jit(solution)/shard_map/ppermute | solution.py:32
  (79 other events, 576.2 us)
Sparse Core Ops, SparseCore 0:
  154.8 131.3 all-reduce.2
